TPU v7x, 512 devices: a whole 4x8x8 slice. The times are simulated.
512 devices in a mesh: kv: 16 (over z, core), ep: 32 (over x, y).
Axes of the slice: x: 4, y: 8, z: 8, core: 2. Of those that a mesh axis runs over, the one named last changes fastest.
Arguments:
- queries: bfloat16 [32, 64, 2048], P('ep'), may hold values from -12 to 12
- new_keys: bfloat16 [32, 64, 512], P('ep'), may hold values from -12 to 12
- new_values: bfloat16 [32, 64, 512], P('ep'), may hold values from -6 to 6
- cache_keys: bfloat16 [32, 64, 128, 512], P('ep', 'kv'), may hold values from -12 to 12
- cache_values: bfloat16 [32, 64, 128, 512], P('ep', 'kv'), may hold values from -10 to 10
- page_table: int32 [32, 64], P('ep'), may hold values from 0 to 63, each once within a row
- cached_len: int32 [32], P('ep'), may hold values from 1 to 8192, 65536 in all
- moe_rows: bfloat16 [1024, 4096], P('ep'), may hold values from -6 to 6
- expert_ids: int32 [1024, 2], P('ep'), may hold values from 0 to 7, all different within a row; in each aligned block of 32 rows (0 to 31, 32 to 63, ...) at most 16 rows name the same one
- gate_probs: float32 [1024, 2], P('ep'), may hold values from 0.1 to 0.9
- w_gate: bfloat16 [32, 4096, 2048], P('ep', None, 'kv'), may hold values from -0.09375 to 0.09375
- w_up: bfloat16 [32, 4096, 2048], P('ep', None, 'kv'), may hold values from -0.09375 to 0.09375
- w_down: bfloat16 [32, 2048, 4096], P('ep', 'kv'), may hold values from -0.09375 to 0.09375
Outputs:
- attn_out: bfloat16 [32, 64, 2048], P('ep')
- moe_out: bfloat16 [1024, 4096], P('ep', 'kv')
Inputs may be any that keep to these rules, and one draw needn't show every extreme that they name: `page_table`: each row is a permutation of the 64 slots of its request. `cached_len`: cached positions at or past a request's length hold no data. `expert_ids`: each row names 2 different experts; among the 32 rows of one ep index no expert is named more than 16 times, and this bound is reached.
All inputs are finite; a program needn't handle non-finite values. No bound on the sum of `cached_len` on one device may be relied on, other than what follows from the above.
Results may differ from a plain program's by a relative error of at most 0.0085.
Values may be sent and summed in bfloat16 or wider, within the bound.
No kernel may reach another device: no remote copies, remote signals or barrier semaphores. Data moves between devices by JAX's collectives and lax.ppermute only.
A program may use at most 128 MiB of HBM per device.

v0:
```python
import math
import jax
import jax.numpy as jnp
from jax import lax
from jax.sharding import PartitionSpec as P

HD = 128
EXPERTS = 8
TOP = 2
HQ = 16
KVH = 4
PAGE = 128
POOL_DEV = 4
CAP = 16
ROPE_BASE = 10000.0
MASKED = -1e30


def merged(part, axis, combine):
    gathered = jax.tree.map(lambda a: lax.all_gather(a, axis), part)

    def take(source):
        return jax.tree.map(lambda a: lax.dynamic_index_in_dim(a, source, 0, False), gathered)

    return lax.fori_loop(
        1, lax.axis_size(axis), lambda source, state: combine(state, take(source)), take(0)
    )


def rotary(values, positions):
    half_width = values.shape[-1] // 2
    indices = jnp.arange(half_width, dtype=jnp.float32)
    frequency = jnp.power(ROPE_BASE, -2.0 * indices / values.shape[-1])
    angles = positions.astype(jnp.float32)[:, None] * frequency[None, :]
    cosine = jnp.cos(angles)[:, None, :]
    sine_part = jnp.sin(angles)[:, None, :]
    lower_half = values[..., :half_width]
    upper_half = values[..., half_width:]
    return jnp.concatenate(
        [
            lower_half * cosine - upper_half * sine_part,
            upper_half * cosine + lower_half * sine_part,
        ],
        axis=-1,
    )


def combine_parts(first, second):
    high_first, total_first, blend_first = first
    high_second, total_second, blend_second = second
    highest = jnp.maximum(high_first, high_second)
    factor_first = jnp.exp(high_first - highest)
    factor_second = jnp.exp(high_second - highest)
    row_count, head_count = highest.shape
    blended = (
        blend_first.reshape(row_count, head_count, -1) * factor_first[..., None]
        + blend_second.reshape(row_count, head_count, -1) * factor_second[..., None]
    )
    return (
        highest,
        total_first * factor_first + total_second * factor_second,
        blended.reshape(blend_first.shape),
    )


def on_device(
    queries,
    new_keys,
    new_values,
    cache_keys,
    cache_values,
    page_table,
    cached_len,
    moe_rows,
    expert_ids,
    gate_probs,
    w_gate,
    w_up,
    w_down,
):
    kv_index = lax.axis_index("kv")
    kv_count = lax.axis_size("kv")
    all_rows = queries.shape[1]
    block_rows = all_rows // kv_count
    length = cached_len[0]
    group_size = HQ // KVH
    score_scale = 1.0 / math.sqrt(HD)
    slot_ids = kv_index * POOL_DEV + jnp.arange(POOL_DEV, dtype=jnp.int32)
    matches = (page_table[0][:, None] == slot_ids[None, :]).astype(jnp.int32)
    page_index = jnp.sum(
        matches * jnp.arange(page_table.shape[1], dtype=jnp.int32)[:, None], axis=0
    )
    cached_pos = (page_index[:, None] * PAGE + jnp.arange(PAGE, dtype=jnp.int32)[None, :]).reshape(
        -1
    )
    block_start = kv_index * block_rows
    own_pos = length + block_start + jnp.arange(block_rows, dtype=jnp.int32)
    key_block = lax.dynamic_slice_in_dim(new_keys[0], block_start, block_rows, 0)
    value_block = lax.dynamic_slice_in_dim(new_values[0], block_start, block_rows, 0)
    own_keys = rotary(key_block.astype(jnp.float32).reshape(block_rows, KVH, HD), own_pos).astype(
        jnp.bfloat16
    )
    local_keys = jnp.concatenate([cache_keys[0].reshape(-1, KVH, HD), own_keys], axis=0)
    local_values = jnp.concatenate(
        [cache_values[0].reshape(-1, KVH, HD), value_block.reshape(block_rows, KVH, HD)], axis=0
    )
    key_pos = jnp.concatenate([cached_pos, own_pos])
    live_keys = jnp.concatenate([cached_pos < length, jnp.ones((block_rows,), jnp.bool_)])
    positions = length + jnp.arange(all_rows, dtype=jnp.int32)
    rotated = rotary(queries[0].astype(jnp.float32).reshape(all_rows, HQ, HD), positions).astype(
        jnp.bfloat16
    )
    grouped = rotated.reshape(all_rows, KVH, group_size, HD)
    scores = (
        jnp.einsum("nkgd,mkd->nkgm", grouped, local_keys, preferred_element_type=jnp.float32)
        * score_scale
    )
    usable = (live_keys[None, :] & (key_pos[None, :] <= positions[:, None]))[:, None, None, :]
    scores = jnp.where(usable, scores, MASKED)
    part_high = jnp.max(scores, axis=-1)
    weights = jnp.where(usable, jnp.exp(scores - part_high[..., None]), 0.0)
    part_total = jnp.sum(weights, axis=-1)
    part_blend = jnp.einsum(
        "nkgm,mkd->nkgd",
        weights.astype(jnp.bfloat16),
        local_values,
        preferred_element_type=jnp.float32,
    )
    partials = (
        part_high.reshape(all_rows, HQ),
        part_total.reshape(all_rows, HQ),
        part_blend.reshape(all_rows, HQ * HD),
    )
    highest, row_total, blended = merged(partials, "kv", combine_parts)
    attn_out = (
        (blended.reshape(all_rows, HQ, HD) / row_total[..., None])
        .reshape(1, all_rows, HQ * HD)
        .astype(jnp.bfloat16)
    )
    ep_count = lax.axis_size("ep")
    share_count = ep_count // EXPERTS
    tok_rows = moe_rows.shape[0]
    slot_total = ep_count * CAP
    flat_ids = expert_ids.reshape(-1)
    one_hot = (flat_ids[:, None] == jnp.arange(EXPERTS, dtype=jnp.int32)[None, :]).astype(jnp.int32)
    earlier = jnp.cumsum(one_hot, axis=0) - one_hot
    slot_rank = jnp.sum(earlier * one_hot, axis=1)
    slot_index = jnp.arange(slot_total, dtype=jnp.int32)
    dest_expert = slot_index // CAP // share_count
    dest_slot = slot_index % CAP
    matched = (flat_ids[None, :] == dest_expert[:, None]) & (
        slot_rank[None, :] == dest_slot[:, None]
    )
    select = jnp.sum(matched.astype(jnp.float32).reshape(slot_total, tok_rows, TOP), axis=2).astype(
        jnp.bfloat16
    )
    weight_map = jnp.sum(
        jnp.where(matched, gate_probs.reshape(-1)[None, :], 0.0).reshape(slot_total, tok_rows, TOP),
        axis=2,
    )
    outgoing = (
        jnp.dot(select, moe_rows, preferred_element_type=jnp.float32)
        .astype(jnp.bfloat16)
        .reshape(ep_count, CAP, -1)
    )
    arrived = lax.all_to_all(outgoing, "ep", split_axis=0, concat_axis=0, tiled=True).reshape(
        slot_total, -1
    )
    gate_proj = jnp.dot(arrived, w_gate[0], preferred_element_type=jnp.float32)
    up_proj = jnp.dot(arrived, w_up[0], preferred_element_type=jnp.float32)
    hidden = (jax.nn.silu(gate_proj) * up_proj).astype(jnp.bfloat16)
    out_width = w_down.shape[2] // kv_count
    down_split = w_down[0].reshape(w_down.shape[1], kv_count, out_width)
    down_cols = lax.all_to_all(down_split, "kv", split_axis=1, concat_axis=0, tiled=True).reshape(
        -1, out_width
    )
    summed = jnp.dot(
        lax.all_gather(hidden, "kv", axis=1, tiled=True),
        down_cols,
        preferred_element_type=jnp.float32,
    )
    returned = (
        lax.all_to_all(
            summed.reshape(ep_count, CAP, -1).astype(jnp.bfloat16),
            "ep",
            split_axis=0,
            concat_axis=0,
            tiled=True,
        )
        .astype(jnp.float32)
        .reshape(slot_total, -1)
    )
    moe_out = jnp.dot(
        weight_map.T, returned, precision=lax.Precision.HIGHEST, preferred_element_type=jnp.float32
    ).astype(jnp.bfloat16)
    return (attn_out, moe_out)


def solution(mesh):
    return jax.shard_map(
        on_device,
        mesh=mesh,
        in_specs=(
            P("ep", None, None),
            P("ep", None, None),
            P("ep", None, None),
            P("ep", "kv", None, None),
            P("ep", "kv", None, None),
            P("ep", None),
            P("ep"),
            P("ep", None),
            P("ep", None),
            P("ep", None),
            P("ep", None, "kv"),
            P("ep", None, "kv"),
            P("ep", "kv", None),
        ),
        out_specs=(P("ep", None, None), P("ep", "kv")),
        check_vma=False,
    )
```

profile of v0, /device:TPU:1, one launch (start us, length us, event | category | flops | bytes accessed | tf_op | source)
XLA Modules:
  0.0 284.0 jit_solution(5398753687239622973)
XLA Ops:
  7.2 0.8 copy.56
  8.7 0.8 convert_reduce_fusion
  9.6 2.2 convolution_convert_fusion
  11.8 102.2 %all_to_all.25 = bf16[32,16,4096]{2,1,0:T(8,128)(2,1)S(1)} all-to-all(bf16[32,16,4096]{2,1,0:T(8,128)(2,1)S(1)} %bitcast.135), channel_id=1, replica_groups=mesh['kv'=16,'ep'=32] {'ep'}, dimensions={0} | all-to-all | bytes 8388608 | tf_op jit(solution)/shard_map/all_to_all | solution.py:166
  113.9 1.3 fusion.14
  115.2 1.9 fusion.12
  118.2 0.9 copy.50
  119.7 0.7 bitcast_convert_fusion
  120.9 0.2 fusion.50
  121.1 0.3 subtract_convert_fusion
  121.5 0.8 fusion.3
  122.3 0.8 fusion.9
  123.0 0.8 copy-done.1
  123.8 0.3 copy.54
  124.2 1.0 all_gather_reshape.11
  125.2 0.2 copy.67
  125.5 1.3 copy.58
  126.8 15.6 %all-to-all-start.1 = ((bf16[128,16,256]{2,0,1:T(8,128)(2,1)}), bf16[128,16,256]{2,0,1:T(8,128)(2,1)S(1)}, u32[]{:S(2)}, u32[]{:S(2)}) async-start(bf16[128,16,256]{2,0,1:T(8,128)(2,1)} %copy.58), calls=%async_computation.1 | async-start | bytes 2097152 | tf_op jit(solution)/shard_map/all_to_all | solution.py:174
  142.3 2.6 fusion.5
  145.0 28.9 %all-to-all-done.1 = bf16[128,16,256]{2,0,1:T(8,128)(2,1)S(1)} async-done(((bf16[128,16,256]{2,0,1:T(8,128)(2,1)}), bf16[128,16,256]{2,0,1:T(8,128)(2,1)S(1)}, u32[]{:S(2)}, u32[]{:S(2)}) %all-to-all-start.1) | async-done | bytes 1048608 | tf_op jit(solution)/shard_map/all_to_all | solution.py:174
  173.9 6.0 %all-gather.5.cloned.1.call-done = bf16[512,2048]{1,0:T(8,128)(2,1)} async-done(((bf16[512,128]{1,0:T(8,128)(2,1)}), bf16[512,2048]{1,0:T(8,128)(2,1)}) %all-gather.5.cloned.1.call-update) | async-done | bytes 2097168 | tf_op jit(solution)/shard_map/all_gather | solution.py:178
  179.9 3.0 %convolution_convert_fusion.1 = bf16[32,16,256]{2,1,0:T(8,128)(2,1)} fusion(bf16[32,16,2048]{2,1,0:T(8,128)(2,1)} %bitcast.146, bf16[2048,256,1]{1,0,2:T(8,128)(2,1)S(1)} %bitcast.140), kind=kOutput, calls=%fused_computation.18 | convolution fusion | flops 537001984 | bytes 3407872 | tf_op jit(solution)/shard_map/dot_general | solution.py:177
  182.9 10.4 %all-to-all-start.2 = ((bf16[32,16,256]{2,1,0:T(8,128)(2,1)}), bf16[32,16,256]{2,1,0:T(8,128)(2,1)S(1)}, u32[]{:S(2)}, u32[]{:S(2)}) async-start(bf16[32,16,256]{2,1,0:T(8,128)(2,1)} %convolution_convert_fusion.1), calls=%async_computation.2 | async-start | bytes 524288 | tf_op jit(solution)/shard_map/all_to_all | solution.py:183
  193.4 18.7 %all_gather.12 = f32[16,64,16]{1,2,0:T(8,128)S(1)} all-gather(f32[1,64,16]{1,2,0:T(8,128)S(1)} %bitcast.144), channel_id=1, replica_groups=mesh['kv'=16,'ep'=32] {'kv'}, dimensions={0}, use_global_device_ids=true | all-gather | bytes 69632 | tf_op jit(solution)/shard_map/all_gather | solution.py:20
  212.1 15.8 %all_gather.13 = f32[16,64,16]{1,2,0:T(8,128)S(1)} all-gather(f32[1,64,16]{1,2,0:T(8,128)S(1)} %bitcast.145), channel_id=1, replica_groups=mesh['kv'=16,'ep'=32] {'kv'}, dimensions={0}, use_global_device_ids=true | all-gather | bytes 69632 | tf_op jit(solution)/shard_map/all_gather | solution.py:20
  227.9 0.9 convolution_convert_fusion.2
  228.8 13.1 %all-gather.3.cloned.1.call-done = f32[16,64,2048]{2,1,0:T(8,128)} async-done(((f32[1,64,2048]{2,1,0:T(8,128)}), f32[16,64,2048]{2,1,0:T(8,128)}) %all-gather.3.cloned.1.call-update) | async-done | bytes 8388624 | tf_op jit(solution)/shard_map/all_gather | solution.py:20
  241.8 1.1 slice_bitcast_fusion
  242.9 33.0 %while.19 = (s32[]{:T(128)}, f32[64,16]{0,1:T(8,128)S(1)}, f32[64,16]{0,1:T(8,128)S(1)}, f32[64,2048]{1,0:T(8,128)S(1)}, f32[16,64,16]{1,2,0:T(8,128)S(1)}, /*in...) while((s32[]{:T(128)}, f32[64,16]{0,1:T(8,128)S(1)}, ...), condition=%wide.region_4.5_spmd, body=%wide.region_3.4_spmd.sunk | while | flops 399365 | bytes 3727511 | solution.py:25
  243.5 1.6 fusion.62
  245.5 0.2 mul.309
  245.7 1.6 fusion.62
  247.7 0.2 mul.309
  247.9 1.6 fusion.62
  249.9 0.2 mul.309
  250.1 1.6 fusion.62
  252.3 1.6 fusion.62
  254.5 1.6 fusion.62
  256.7 1.6 fusion.62
  258.9 1.6 fusion.62
  261.1 1.6 fusion.62
  263.3 1.6 fusion.62
  265.5 1.6 fusion.62
  267.7 1.6 fusion.62
  269.9 1.6 fusion.62
  272.1 1.6 fusion.62
  274.3 1.6 fusion.62
  276.2 0.9 fusion.27
  (124 shorter events, 10.4 us)
Async XLA Ops:
  7.2 106.8 %copy-start = (bf16[1,4096,128]{2,1,0:T(8,128)(2,1)S(1)}, bf16[1,4096,128]{2,1,0:T(8,128)(2,1)}, u32[]{:S(2)}) copy-start(bf16[1,4096,128]{2,1,0:T(8,128)(2,1)} %param.25) | copy-start | bytes 3145732
  7.2 172.8 %all-gather.5.cloned.1.call-start = ((), (), s32[]{:S(2)}) async-start(), calls=%async_computation.4 | async-start | bytes 2228224 | tf_op jit(solution)/shard_map/all_gather | solution.py:178
  113.9 1.3 copy-start.7
  115.2 2.7 copy-start.6
  115.2 2.9 %copy-start.3 = (bf16[1,4,128,512]{3,2,1,0:T(8,128)(2,1)S(1)}, bf16[1,4,128,512]{3,2,1,0:T(8,128)(2,1)}, u32[]{:S(2)}) copy-start(bf16[1,4,128,512]{3,2,1,0:T(8,128)(2,1)} %param.18) | copy-start | bytes 1572868
  117.1 1.9 copy-start.4
  117.2 124.7 %all-gather.3.cloned.1.call-start = ((), (), s32[]{:S(2)}) async-start(), calls=%async_computation.3 | async-start | bytes 8912896 | tf_op jit(solution)/shard_map/all_gather | solution.py:20
  118.0 1.3 copy-start.8
  119.2 2.3 copy-start.5
  122.3 1.6 copy-start.1
  123.8 1.4 copy-start.2
  126.8 47.1 %all-to-all-start.1 = ((bf16[128,16,256]{2,0,1:T(8,128)(2,1)}), bf16[128,16,256]{2,0,1:T(8,128)(2,1)S(1)}, u32[]{:S(2)}, u32[]{:S(2)}) async-start(bf16[128,16,256]{2,0,1:T(8,128)(2,1)} %copy.58), calls=%async_computation.1 | async-start | bytes 2097152 | tf_op jit(solution)/shard_map/all_to_all | solution.py:174
  182.9 45.0 %all-to-all-start.2 = ((bf16[32,16,256]{2,1,0:T(8,128)(2,1)}), bf16[32,16,256]{2,1,0:T(8,128)(2,1)S(1)}, u32[]{:S(2)}, u32[]{:S(2)}) async-start(bf16[32,16,256]{2,1,0:T(8,128)(2,1)} %convolution_convert_fusion.1), calls=%async_computation.2 | async-start | bytes 524288 | tf_op jit(solution)/shard_map/all_to_all | solution.py:183
Sparse Core Ops, SparseCore 0:
  117.3 62.6 all-gather.4
  182.1 59.7 all-gather.2
where the time goes:
time: 285 us; the launch traced here: 284 us
  blocking collectives  137 us (48%)
  waiting for transfers between devices  48.1 us (17%)
  other arithmetic  30.8 us (11%)
  starting transfers between devices  26.1 us (9%)
  local copies, waits for them, and re-layouts  16 us (6%)
  between operations  15 us (5%)
  matrix products  10.8 us (4%)
    all_to_all x1, blocking collectives, on_device(): lax.all_to_all(outgoing, 'ep', split_axis=0, concat_axis=0, tiled=True)  102 us
    all_gather x2, blocking collectives, merged(): gathered = jax.tree.map(lambda a: lax.all_gather(a, axis), part)  34.5 us
    all_to_all x1, waiting for transfers between devices, on_device(): lax.all_to_all(down_split, 'kv', split_axis=1, concat_axis=0, tiled=True)  28.9 us
    add x15, other arithmetic, combine_parts(): blend_first.reshape(row_count, head_count, -1) * factor_first[..., None]  23.9 us
    all_to_all x1, starting transfers between devices, on_device(): lax.all_to_all(down_split, 'kv', split_axis=1, concat_axis=0, tiled=True)  15.6 us
    all_gather x1, waiting for transfers between devices, merged(): gathered = jax.tree.map(lambda a: lax.all_gather(a, axis), part)  13.1 us
    all_to_all x1, starting transfers between devices, on_device(): lax.all_to_all(summed.reshape(ep_count, CAP, -1).astype(jnp.bfloat16), 'e...  10.4 us
    all_gather x1, waiting for transfers between devices, on_device(): lax.all_gather(hidden, 'kv', axis=1, tiled=True)  6.04 us
  transfers between devices with their start and end apart: 4, of which 3 were waited for; matrix products, arithmetic and copies ran while one was open for 5% of the time, Pallas kernels for 0%

commit v1 on v0

--- a/solution.py
+++ b/solution.py
@@ -14,6 +14,18 @@
 CAP = 16
 ROPE_BASE = 10000.0
 MASKED = -1e30
+
+
+def lead_grid_up(local_block, along_dim):
+    return jnp.concatenate(
+        jax.lax.all_to_all(
+            jnp.stack(tuple((local_block for _ in range(jax.lax.axis_size("kv"))))),
+            axis_name="kv",
+            split_axis=0,
+            concat_axis=0,
+        ),
+        along_dim,
+    )
 
 
 def merged(part, axis, combine):
@@ -174,11 +186,7 @@
     down_cols = lax.all_to_all(down_split, "kv", split_axis=1, concat_axis=0, tiled=True).reshape(
         -1, out_width
     )
-    summed = jnp.dot(
-        lax.all_gather(hidden, "kv", axis=1, tiled=True),
-        down_cols,
-        preferred_element_type=jnp.float32,
-    )
+    summed = jnp.dot(lead_grid_up(hidden, 1), down_cols, preferred_element_type=jnp.float32)
     returned = (
         lax.all_to_all(
             summed.reshape(ep_count, CAP, -1).astype(jnp.bfloat16),

time: 285 us -> 305 us (1.070)
  blocking collectives: 137 us -> 29.7 us
  waiting for transfers between devices: 48.1 us -> 149 us
  starting transfers between devices: 26.1 us -> 36.2 us
  local copies, waits for them, and re-layouts: 16 us -> 25.4 us
  matrix products: 10.8 us -> 17.2 us
    all_to_all x0 -> x2, waiting for transfers between devices: none -> 129 us  [the longest x1 82.6 us: on_device(): lax.all_to_all(outgoing, 'ep', split_axis=0, concat_axis=0, tiled=True)]
    all_to_all x1 -> x0, blocking collectives: 102 us -> none  [on_device(): lax.all_to_all(outgoing, 'ep', split_axis=0, concat_axis=0, tiled=True)]
    all_to_all x0 -> x2, starting transfers between devices: none -> 26.5 us  [the longest x1 15.7 us: lead_grid_up(): jax.lax.all_to_all(jnp.stack(tuple((local_block for _ in range(jax.lax.ax...]
    all_gather x1, waiting for transfers between devices: 13.1 us -> 0.01 us  [merged(): gathered = jax.tree.map(lambda a: lax.all_gather(a, axis), part)]
    all_to_all x1, starting transfers between devices: 15.6 us -> 4.85 us  [on_device(): lax.all_to_all(down_split, 'kv', split_axis=1, concat_axis=0, tiled=True)]
    all_to_all x1, waiting for transfers between devices: 28.9 us -> 19.9 us  [on_device(): lax.all_to_all(down_split, 'kv', split_axis=1, concat_axis=0, tiled=True)]
    all_gather x1 -> x0, waiting for transfers between devices: 6.04 us -> none  [on_device(): lax.all_gather(hidden, 'kv', axis=1, tiled=True)]
    all_to_all x1, starting transfers between devices: 10.4 us -> 4.79 us  [on_device(): lax.all_to_all(summed.reshape(ep_count, CAP, -1).astype(jnp.bfloat16), 'e...]
  transfers between devices with their start and end apart: 4 -> 5, of which waited for: 3 -> 3; matrix products, arithmetic and copies ran while one was open for 5% -> 10% of each run, Pallas kernels for 0% -> 0%
where the time goes in v1:
time: 305 us; the launch traced here: 304 us
  waiting for transfers between devices  149 us (49%)
  starting transfers between devices  36.2 us (12%)
  other arithmetic  30.8 us (10%)
  blocking collectives  29.7 us (10%)
  local copies, waits for them, and re-layouts  25.4 us (8%)
  matrix products  17.2 us (6%)
  between operations  15 us (5%)
    all_to_all x1, waiting for transfers between devices, on_device(): lax.all_to_all(outgoing, 'ep', split_axis=0, concat_axis=0, tiled=True)  82.6 us
    all_to_all x1, waiting for transfers between devices, lead_grid_up(): jax.lax.all_to_all(jnp.stack(tuple((local_block for _ in range(jax.lax.ax...  46.3 us
    all_gather x2, blocking collectives, merged(): gathered = jax.tree.map(lambda a: lax.all_gather(a, axis), part)  29.7 us
    add x15, other arithmetic, combine_parts(): blend_first.reshape(row_count, head_count, -1) * factor_first[..., None]  23.9 us
    all_to_all x1, waiting for transfers between devices, on_device(): lax.all_to_all(down_split, 'kv', split_axis=1, concat_axis=0, tiled=True)  19.9 us
    all_to_all x1, starting transfers between devices, lead_grid_up(): jax.lax.all_to_all(jnp.stack(tuple((local_block for _ in range(jax.lax.ax...  15.7 us
    all_to_all x1, starting transfers between devices, on_device(): lax.all_to_all(outgoing, 'ep', split_axis=0, concat_axis=0, tiled=True)  10.7 us
  transfers between devices with their start and end apart: 5, of which 3 were waited for; matrix products, arithmetic and copies ran while one was open for 10% of the time, Pallas kernels for 0%

profile of v1, /device:TPU:1, one launch (start us, length us, event | category | flops | bytes accessed | tf_op | source)
XLA Modules:
  0.0 303.7 jit_solution(1586962077159604792)
XLA Ops:
  7.2 0.8 copy.57
  8.7 0.8 convert_reduce_fusion
  9.5 4.2 %convolution_convert_fusion = bf16[512,4096]{1,0:T(8,128)(2,1)} fusion(bf16[32,4096]{1,0:T(8,128)(2,1)} %param.22, bf16[512,32]{0,1:T(8,128)(2,1)S(1)} %get-tuple-element.181), kind=kOutput, calls=%fused_computation.9 | convolution fusion | flops 136314880 | bytes 4489216 | tf_op jit(solution)/shard_map/dot_general | solution.py:174
  13.7 10.7 %all-to-all-start = ((bf16[32,16,4096]{2,1,0:T(8,128)(2,1)}), bf16[32,16,4096]{2,1,0:T(8,128)(2,1)}, u32[]{:S(2)}, u32[]{:S(2)}) async-start(bf16[32,16,4096]{2,1,0:T(8,128)(2,1)} %bitcast.133), calls=%async_computation | async-start | bytes 8388608 | tf_op jit(solution)/shard_map/all_to_all | solution.py:178
  26.4 0.9 copy.51
  27.3 1.2 reshape_squeeze.10
  28.6 0.7 bitcast_convert_fusion
  29.4 0.3 subtract_convert_fusion
  29.8 1.8 fusion.3
  31.6 0.8 fusion.9
  32.4 0.7 copy-done.1
  33.4 1.0 all_gather_reshape.11
  34.5 82.6 %all-to-all-done = bf16[32,16,4096]{2,1,0:T(8,128)(2,1)} async-done(((bf16[32,16,4096]{2,1,0:T(8,128)(2,1)}), bf16[32,16,4096]{2,1,0:T(8,128)(2,1)}, u32[]{:S(2)}, u32[]{:S(2)}) %all-to-all-start) | async-done | bytes 4194336 | tf_op jit(solution)/shard_map/all_to_all | solution.py:178
  117.1 3.5 %fusion.14 = f32[512,128]{1,0:T(8,128)S(1)} fusion(bf16[512,4096]{1,0:T(8,128)(2,1)} %bitcast.24, bf16[1,4096,128]{2,1,0:T(8,128)(2,1)S(1)} %copy-done), kind=kOutput, calls=%fused_computation.23 | convolution fusion | flops 536870912 | bytes 5505024 | tf_op jit(solution)/shard_map/dot_general | solution.py:181
  120.6 3.4 %fusion.12 = bf16[512,128]{1,0:T(8,128)(2,1)S(1)} fusion(bf16[512,4096]{1,0:T(8,128)(2,1)} %bitcast.24, bf16[1,4096,128]{2,1,0:T(8,128)(2,1)S(1)} %copy-done.4, f32[512,128]{1,0:T(8,128)S(1)} %fusion.14), kind=kOutput, calls=%fused_computation.20 | convolution fusion | flops 537264128 | bytes 5636096 | tf_op jit(solution)/shard_map/dot_general | solution.py:182
  124.1 1.8 stack.2
  125.8 15.7 %all-to-all-start.1 = ((bf16[16,512,128]{2,1,0:T(8,128)(2,1)}), bf16[16,512,128]{2,1,0:T(8,128)(2,1)S(1)}, u32[]{:S(2)}, u32[]{:S(2)}) async-start(bf16[16,512,128]{2,1,0:T(8,128)(2,1)} %stack.2), calls=%async_computation.1 | async-start | bytes 4194304 | tf_op jit(solution)/shard_map/all_to_all | solution.py:21
  141.6 1.5 copy.69
  143.0 1.3 copy.60
  144.4 46.3 %all-to-all-done.1 = bf16[16,512,128]{2,1,0:T(8,128)(2,1)S(1)} async-done(((bf16[16,512,128]{2,1,0:T(8,128)(2,1)}), bf16[16,512,128]{2,1,0:T(8,128)(2,1)S(1)}, u32[]{:S(2)}, u32[]{:S(2)}) %all-to-all-start.1) | async-done | bytes 2097184 | tf_op jit(solution)/shard_map/all_to_all | solution.py:21
  190.6 4.8 %all-to-all-start.2 = ((bf16[128,16,256]{2,0,1:T(8,128)(2,1)}), bf16[128,16,256]{2,0,1:T(8,128)(2,1)}, u32[]{:S(2)}, u32[]{:S(2)}) async-start(bf16[128,16,256]{2,0,1:T(8,128)(2,1)} %copy.60), calls=%async_computation.2 | async-start | bytes 2097152 | tf_op jit(solution)/shard_map/all_to_all | solution.py:186
  195.5 2.6 fusion.5
  198.1 2.7 copy.59
  200.8 2.8 dot_general.28
  203.6 19.9 %all-to-all-done.2 = bf16[128,16,256]{2,0,1:T(8,128)(2,1)} async-done(((bf16[128,16,256]{2,0,1:T(8,128)(2,1)}), bf16[128,16,256]{2,0,1:T(8,128)(2,1)}, u32[]{:S(2)}, u32[]{:S(2)}) %all-to-all-start.2) | async-done | bytes 1048608 | tf_op jit(solution)/shard_map/all_to_all | solution.py:186
  223.6 2.6 convolution_convert_fusion.1
  226.2 4.8 %all-to-all-start.3 = ((bf16[32,16,256]{2,1,0:T(8,128)(2,1)}), bf16[32,16,256]{2,1,0:T(8,128)(2,1)S(1)}, u32[]{:S(2)}, u32[]{:S(2)}) async-start(bf16[32,16,256]{2,1,0:T(8,128)(2,1)} %convolution_convert_fusion.1), calls=%async_computation.3 | async-start | bytes 524288 | tf_op jit(solution)/shard_map/all_to_all | solution.py:191
  231.0 14.8 %all_gather.9 = f32[16,64,16]{1,2,0:T(8,128)S(1)} all-gather(f32[1,64,16]{1,2,0:T(8,128)S(1)} %bitcast.142), channel_id=1, replica_groups=mesh['kv'=16,'ep'=32] {'kv'}, dimensions={0}, use_global_device_ids=true | all-gather | bytes 69632 | tf_op jit(solution)/shard_map/all_gather | solution.py:32
  245.8 14.8 %all_gather.10 = f32[16,64,16]{1,2,0:T(8,128)S(1)} all-gather(f32[1,64,16]{1,2,0:T(8,128)S(1)} %bitcast.143), channel_id=1, replica_groups=mesh['kv'=16,'ep'=32] {'kv'}, dimensions={0}, use_global_device_ids=true | all-gather | bytes 69632 | tf_op jit(solution)/shard_map/all_gather | solution.py:32
  260.7 0.9 convolution_convert_fusion.2
  261.5 1.1 slice_bitcast_fusion
  262.6 33.0 %while.19 = (s32[]{:T(128)}, f32[64,16]{0,1:T(8,128)S(1)}, f32[64,16]{0,1:T(8,128)S(1)}, f32[64,2048]{1,0:T(8,128)S(1)}, f32[16,64,16]{1,2,0:T(8,128)S(1)}, /*in...) while((s32[]{:T(128)}, f32[64,16]{0,1:T(8,128)S(1)}, ...), condition=%wide.region_4.5_spmd, body=%wide.region_3.4_spmd.sunk | while | flops 399365 | bytes 3727511 | solution.py:37
  263.2 1.6 fusion.62
  265.4 1.6 fusion.62
  267.6 1.6 fusion.62
  269.8 1.6 fusion.62
  272.0 1.6 fusion.62
  274.2 1.6 fusion.62
  276.4 1.6 fusion.62
  278.6 1.6 fusion.62
  280.8 1.6 fusion.62
  283.0 1.6 fusion.62
  285.2 1.6 fusion.62
  287.4 1.6 fusion.62
  289.6 1.6 fusion.62
  291.8 1.6 fusion.62
  294.0 1.6 fusion.62
  295.9 0.9 fusion.27
  (121 shorter events, 11.3 us)
Async XLA Ops:
  7.2 109.9 %copy-start = (bf16[1,4096,128]{2,1,0:T(8,128)(2,1)S(1)}, bf16[1,4096,128]{2,1,0:T(8,128)(2,1)}, u32[]{:S(2)}) copy-start(bf16[1,4096,128]{2,1,0:T(8,128)(2,1)} %param.25) | copy-start | bytes 3145732
  13.7 11.6 %copy-start.5 = (s32[1,64]{1,0:T(1,128)S(1)}, s32[1,64]{1,0:T(1,128)}, u32[]{:S(2)}) copy-start(s32[1,64]{1,0:T(1,128)} %param.20) | copy-start | bytes 772
  13.7 11.9 %copy-start.3 = (bf16[1,64,2048]{2,1,0:T(8,128)(2,1)S(1)}, bf16[1,64,2048]{2,1,0:T(8,128)(2,1)}, u32[]{:S(2)}) copy-start(bf16[1,64,2048]{2,1,0:T(8,128)(2,1)} %param.15) | copy-start | bytes 786436
  13.7 103.4 %all-to-all-start = ((bf16[32,16,4096]{2,1,0:T(8,128)(2,1)}), bf16[32,16,4096]{2,1,0:T(8,128)(2,1)}, u32[]{:S(2)}, u32[]{:S(2)}) async-start(bf16[32,16,4096]{2,1,0:T(8,128)(2,1)} %bitcast.133), calls=%async_computation | async-start | bytes 8388608 | tf_op jit(solution)/shard_map/all_to_all | solution.py:178
  24.4 1.8 copy-start.2
  24.4 237.1 %all-gather.2.cloned.1.call-start = ((), (), s32[]{:S(2)}) async-start(), calls=%async_computation.4 | async-start | bytes 8912896 | tf_op jit(solution)/shard_map/all_gather | solution.py:32
  31.6 1.5 copy-start.1
  117.1 3.5 %copy-start.4 = (bf16[1,4096,128]{2,1,0:T(8,128)(2,1)S(1)}, bf16[1,4096,128]{2,1,0:T(8,128)(2,1)}, u32[]{:S(2)}) copy-start(bf16[1,4096,128]{2,1,0:T(8,128)(2,1)} %param.26) | copy-start | bytes 3145732
  125.8 64.8 %all-to-all-start.1 = ((bf16[16,512,128]{2,1,0:T(8,128)(2,1)}), bf16[16,512,128]{2,1,0:T(8,128)(2,1)S(1)}, u32[]{:S(2)}, u32[]{:S(2)}) async-start(bf16[16,512,128]{2,1,0:T(8,128)(2,1)} %stack.2), calls=%async_computation.1 | async-start | bytes 4194304 | tf_op jit(solution)/shard_map/all_to_all | solution.py:21
  190.6 32.9 %all-to-all-start.2 = ((bf16[128,16,256]{2,0,1:T(8,128)(2,1)}), bf16[128,16,256]{2,0,1:T(8,128)(2,1)}, u32[]{:S(2)}, u32[]{:S(2)}) async-start(bf16[128,16,256]{2,0,1:T(8,128)(2,1)} %copy.60), calls=%async_computation.2 | async-start | bytes 2097152 | tf_op jit(solution)/shard_map/all_to_all | solution.py:186
  226.2 34.5 %all-to-all-start.3 = ((bf16[32,16,256]{2,1,0:T(8,128)(2,1)}), bf16[32,16,256]{2,1,0:T(8,128)(2,1)S(1)}, u32[]{:S(2)}, u32[]{:S(2)}) async-start(bf16[32,16,256]{2,1,0:T(8,128)(2,1)} %convolution_convert_fusion.1), calls=%async_computation.3 | async-start | bytes 524288 | tf_op jit(solution)/shard_map/all_to_all | solution.py:191
Sparse Core Ops, SparseCore 0:
  34.6 64.3 all-gather.1
